TPU v7x, 512 devices: a whole 4x8x8 slice. The times are simulated.
512 devices in a mesh: freq: 16 (over y, core), trace: 32 (over z, x).
Axes of the slice: x: 4, y: 8, z: 8, core: 2. Of those that a mesh axis runs over, the one named last changes fastest.
Arguments:
- traces: bfloat16 [64, 128, 2048], P('trace', 'freq'), may hold values from -20 to 20
- omega: float32 [2, 33, 64, 64], replicated, may hold values from -0.125 to 0.125
Outputs:
- denoised: float32 [64, 128, 2048], P('trace', 'freq')
All inputs are finite; a program needn't handle non-finite values.
Results may differ from a plain program's by a relative error of at most 0.0003.
Values sent between devices are 32-bit elements; how exact they have to be, the bound alone decides.
No kernel may reach another device: no remote copies, remote signals or barrier semaphores. Data moves between devices by JAX's collectives and lax.ppermute only.
A program may use at most 64 MiB of HBM per device.

v0:
```python
import math
import jax
import jax.numpy as jnp
from jax import lax
from jax.sharding import PartitionSpec as P

FREQ_DEV = 1
highest = lax.Precision.HIGHEST


def fourier_tables(samples, freq_total):
    moments = jnp.arange(samples, dtype=jnp.int32)
    bins = jnp.arange(freq_total, dtype=jnp.int32) + 1
    phases = bins[:, None] * moments[None, :] % samples
    angles = phases.astype(jnp.float32) * (2.0 * math.pi / samples)
    return (jnp.cos(angles), jnp.sin(angles))


def anti_counts(spots, length, window, lags):
    counted = jnp.minimum(jnp.minimum(spots + 1, length - spots), min(window, lags))
    return counted.astype(jnp.float32)


def solve_one(factor, right_side):
    return jax.scipy.linalg.cho_solve((factor, True), right_side)


def body(traces, omega):
    rows_dev, cols_dev, samples = traces.shape
    lag_x, lag_y, rank_size = (omega.shape[1], omega.shape[2], omega.shape[3])
    trace_count = lax.axis_size("trace")
    freq_count = lax.axis_size("freq")
    patch_x = rows_dev * trace_count
    patch_y = cols_dev * freq_count
    win_x = patch_x - lag_x + 1
    win_y = patch_y - lag_y + 1
    freq_total = FREQ_DEV * freq_count
    own_rows = win_x // trace_count
    own_lags = lag_y // trace_count
    position = lax.axis_index("trace")
    cosine_table, sine_table = fourier_tables(samples, freq_total)
    norm_scale = 1.0 / math.sqrt(samples)
    forward = jnp.stack([cosine_table.T, -sine_table.T], axis=1) * norm_scale
    spectrum = jnp.einsum("xyt,tpk->xypk", traces.astype(jnp.float32), forward, precision=highest)
    spectrum = lax.all_to_all(spectrum, "freq", split_axis=3, concat_axis=1, tiled=True)
    slices = jnp.transpose(spectrum, (3, 2, 0, 1))
    whole_slices = lax.all_gather(slices, "trace", axis=2, tiled=True)
    freq_dev = whole_slices.shape[0]
    first_row = position * own_rows
    row_slabs = jnp.stack([lax.dynamic_slice_in_dim(whole_slices, first_row + 0, lag_x, 2)], axis=1)
    hankel = jnp.stack([row_slabs[..., anchor : anchor + lag_y] for anchor in range(win_y)], axis=3)
    hankel_flat = hankel.reshape(freq_dev, own_rows * 2 * win_y, lag_x * lag_y)
    omega_flat = omega.reshape(2, lag_x * lag_y, rank_size)
    products = jnp.einsum("fnm,smq->fnsq", hankel_flat, omega_flat, precision=highest)
    products = products.reshape(freq_dev, own_rows, 2, win_y, 2, rank_size)
    sketch_re = products[:, :, 0, :, 0] - products[:, :, 1, :, 1]
    sketch_im = products[:, :, 0, :, 1] + products[:, :, 1, :, 0]
    own_sketch = jnp.transpose(jnp.concatenate([sketch_re, sketch_im], -1), (1, 0, 2, 3))
    sketch = lax.all_gather(own_sketch, "trace", axis=0, tiled=True)
    inner = lax.psum(
        jnp.einsum("afbp,afbq->fpq", own_sketch, own_sketch, precision=highest), "trace"
    )
    lag_start = position * own_lags
    hankel_blocks = []
    for offset in range(own_lags):
        band = lax.dynamic_slice_in_dim(whole_slices, lag_start + offset, win_y, 3)
        hankel_blocks.append(
            jnp.stack([band[:, :, anchor : anchor + win_x] for anchor in range(lag_x)], axis=2)
        )
    columns = jnp.stack(hankel_blocks, axis=1).reshape(
        freq_dev, own_lags * 2 * lag_x, win_x * win_y
    )
    flat_sketch = jnp.transpose(sketch, (1, 0, 2, 3)).reshape(
        freq_dev, win_x * win_y, 2 * rank_size
    )
    project = jnp.einsum("fnm,fmq->fnq", columns, flat_sketch, precision=highest).reshape(
        freq_dev, own_lags, 2, lag_x, 2 * rank_size
    )
    proj_re = jnp.transpose(
        project[:, :, 0, :, :rank_size] + project[:, :, 1, :, rank_size:], (0, 3, 1, 2)
    )
    proj_im = jnp.transpose(
        project[:, :, 1, :, :rank_size] - project[:, :, 0, :, rank_size:], (0, 3, 1, 2)
    )
    gram_re = inner[:, :rank_size, :rank_size] + inner[:, rank_size:, rank_size:]
    gram_im = inner[:, :rank_size, rank_size:] - inner[:, rank_size:, :rank_size]
    real_gram = jnp.concatenate(
        [jnp.concatenate([gram_re, -gram_im], 2), jnp.concatenate([gram_im, gram_re], 2)], 1
    )
    right_side = jnp.concatenate([proj_re, proj_im], 1).reshape(
        freq_dev, 2 * rank_size, own_lags * lag_x
    )
    factor = jnp.linalg.cholesky(real_gram)
    solved = jax.vmap(solve_one)(factor, right_side)
    mix_re = solved[:, :rank_size]
    mix_im = solved[:, rank_size:]
    mix_real = jnp.concatenate([mix_re, -mix_im], 1).reshape(
        freq_dev, 2 * rank_size, own_lags, lag_x
    )
    mix_imag = jnp.concatenate([mix_im, mix_re], 1).reshape(
        freq_dev, 2 * rank_size, own_lags, lag_x
    )
    mixing = jnp.stack([mix_real, mix_imag], axis=3)
    sketch_cols = jnp.transpose(sketch, (1, 2, 3, 0))
    lowrank = jnp.einsum("fqezc,fbqa->fbezca", mixing, sketch_cols, precision=highest)
    target = (
        jnp.arange(lag_x, dtype=jnp.int32)[:, None] + jnp.arange(win_x, dtype=jnp.int32)[None, :]
    ).reshape(-1)
    diagonal = (target[:, None] == jnp.arange(patch_x, dtype=jnp.int32)[None, :]).astype(
        jnp.float32
    )
    spread = jnp.dot(lowrank.reshape(-1, lag_x * win_x), diagonal, precision=highest).reshape(
        freq_dev, win_y, own_lags, 2, patch_x
    )
    partial_value = jnp.zeros((patch_x, freq_dev, 2, patch_y), jnp.float32)
    zero_index = jnp.zeros((), jnp.int32)
    for offset in range(own_lags):
        band_block = jnp.transpose(spread[:, :, offset], (3, 0, 2, 1))
        partial_value = partial_value + lax.dynamic_update_slice(
            jnp.zeros_like(partial_value),
            band_block,
            (zero_index, zero_index, zero_index, lag_start + offset),
        )
    averaged = lax.psum_scatter(partial_value, "trace", scatter_dimension=0, tiled=True)
    spots_x = position * rows_dev + jnp.arange(rows_dev, dtype=jnp.int32)
    spots_y = jnp.arange(patch_y, dtype=jnp.int32)
    counts = (
        anti_counts(spots_x, patch_x, win_x, lag_x)[:, None, None, None]
        * anti_counts(spots_y, patch_y, win_y, lag_y)[None, None, None, :]
    )
    averaged = averaged / counts
    returned = lax.all_to_all(averaged, "freq", split_axis=3, concat_axis=1, tiled=True)
    inverse = jnp.stack([cosine_table, -sine_table], axis=1) * (2.0 * norm_scale)
    return jnp.einsum("xkpy,kpt->xyt", returned, inverse, precision=highest)


def solution(mesh):
    return jax.shard_map(
        body,
        mesh=mesh,
        in_specs=(P("trace", "freq", None), P()),
        out_specs=P("trace", "freq", None),
        check_vma=False,
    )
```

profile of v0, /device:TPU:1, one launch (start us, length us, event | category | flops | bytes accessed | tf_op | source)
XLA Modules:
  0.0 583.4 jit_solution(9340026111584924302)
XLA Ops:
  7.2 1.4 convolution_bitcast_fusion.5
  9.3 10.1 %all-to-all-start = ((f32[2,8,2,16]{1,0,2,3:T(2,128)}), f32[2,8,2,16]{1,0,2,3:T(2,128)S(1)}, u32[]{:S(2)}, u32[]{:S(2)}) async-start(f32[2,8,2,16]{1,0,2,3:T(2,128)} %copy.367), calls=%async_computation | async-start | bytes 65536 | tf_op jit(solution)/shard_map/all_to_all | solution.py:45
  19.5 7.4 %all-to-all-done = f32[2,8,2,16]{1,0,2,3:T(2,128)S(1)} async-done(((f32[2,8,2,16]{1,0,2,3:T(2,128)}), f32[2,8,2,16]{1,0,2,3:T(2,128)S(1)}, u32[]{:S(2)}, u32[]{:S(2)}) %all-to-all-start) | async-done | bytes 2080 | tf_op jit(solution)/shard_map/all_to_all | solution.py:45
  27.0 41.2 %all_gather.6 = f32[1,2,64,128]{3,1,0,2:T(2,128)S(1)} all-gather(f32[1,2,2,128]{3,1,0,2:T(2,128)S(1)} %bitcast.277), channel_id=1, replica_groups=mesh['freq'=16,'trace'=32] {'trace'}, dimensions={2}, use_global_device_ids=true | all-gather | bytes 67584 | tf_op jit(solution)/shard_map/all_gather | solution.py:47
  68.2 1.6 fusion.69
  69.8 1.4 fusion.68
  71.9 1.0 fusion.70
  73.0 0.8 copy.379
  74.4 0.8 copy.380
  75.9 0.8 copy.381
  77.3 0.8 copy.382
  78.8 0.8 copy.383
  80.2 0.8 copy.384
  81.7 0.8 copy.385
  83.1 0.8 copy.386
  84.6 0.8 copy.387
  86.0 0.8 copy.388
  87.5 0.8 copy.389
  88.9 0.8 copy.390
  90.4 0.8 copy.391
  91.8 0.8 copy.392
  93.3 0.8 copy.393
  94.7 0.8 copy.394
  96.2 0.8 copy.395
  97.6 0.8 copy.396
  99.1 0.8 copy.397
  133.9 9.0 %stack.490 = f32[2,65,2112]{2,1,0:T(8,128)S(1)} concatenate(f32[2,1,2112]{2,1,0:T(1,128)} %stack.562, f32[2,1,2112]{2,1,0:T(1,128)} %stack.563, f32[2,1,2112]{2,1,0:T(1,128)} %stack.564, f32[2,1,2112]{2,1,0:T(1,128)} %stack.565, f32[2,1,2112]{2,1,0:T(1,128)} %stack.566, f32[2,1,2112]{2,1,0:T(1,128)} %stack.567, f32[2,1,2112]{2,1,0:T(1,128)} %stack.568, f32[2,1,2112]{2,1,0:T(1,128)} %stack.569, ...), dimensions={1} | concatenate | bytes 2196480 | tf_op jit(solution)/shard_map/stack | solution.py:51
  142.9 3.6 fusion.6
  146.6 0.9 convolution_bitcast_fusion.3
  149.8 1.2 constant_dynamic-slice_fusion.65
  163.3 1.8 constant_dynamic-slice_fusion.47
  199.0 5.5 stack.524
  204.6 6.3 %stack.558 = f32[1,2,33,2080]{3,2,1,0:T(8,128)} concatenate(f32[1,2,1,2080]{3,2,1,0:T(1,128)S(1)} %copy-done.37, f32[1,2,1,2080]{3,2,1,0:T(1,128)} %stack.526, f32[1,2,1,2080]{3,2,1,0:T(1,128)} %stack.527, f32[1,2,1,2080]{3,2,1,0:T(1,128)} %stack.528, f32[1,2,1,2080]{3,2,1,0:T(1,128)S(1)} %copy-done.48, f32[1,2,1,2080]{3,2,1,0:T(1,128)S(1)} %copy-done.49, ...), dimensions={2} | concatenate | bytes 1098240 | tf_op jit(solution)/shard_map/stack | solution.py:68
  211.0 89.0 %all-reduce.4.cloned.1.call-done = f32[1,128,128]{1,2,0:T(8,128)} async-done(((f32[1,128,128]{1,2,0:T(8,128)}), f32[1,128,128]{1,2,0:T(8,128)}) %all-reduce.4.cloned.1.call-update) | async-done | bytes 65552 | tf_op jit(solution)/shard_map/psum | solution.py:60
  299.9 0.9 fusion.66
  301.2 11.9 %custom-call.11 = f32[1,128,128]{2,1,0:T(8,128)S(1)} custom-call(f32[1,128,128]{2,1,0:T(8,128)S(1)} %fusion.46), custom_call_target="Cholesky" | custom-call | tf_op jit(solution)/shard_map/jit(cholesky)/cholesky | solution.py:93
  314.4 9.8 %custom-call.12 = f32[1,1,128,128]{2,3,1,0:T(8,128)S(1)} custom-call(f32[1,1,128,128]{3,2,1,0:T(8,128)S(1)} %fusion.41), custom_call_target="InvertDiagBlocksLowerTriangular" | custom-call | tf_op jit(solution)/shard_map/vmap(jit(_cho_solve))/triangular_solve | solution.py:25
  324.2 58.3 %all-gather.2.cloned.1.call-done = f32[32,1,65,128]{3,1,2,0:T(1,128)} async-done(((f32[1,1,65,128]{3,1,2,0:T(1,128)}), f32[32,1,65,128]{3,1,2,0:T(1,128)}) %all-gather.2.cloned.1.call-update) | async-done | bytes 1064976 | tf_op jit(solution)/shard_map/all_gather | solution.py:59
  382.6 3.1 fusion.9
  386.6 5.1 convolution_bitcast_fusion.1
  391.8 6.0 %copy.575 = f32[1,65,2,2,33,32]{1,5,4,3,2,0:T(8,128)} copy(f32[1,65,2,2,33,32]{4,5,3,2,1,0:T(8,128)} %convolution_bitcast_fusion.1) | data formatting | bytes 2196480 | tf_op jit(solution)/shard_map/fqezc,fbqa->fbezca/transpose | solution.py:105
  397.8 2.6 convolution_bitcast_fusion.2
  402.2 1.3 dynamic-slice.1
  404.1 149.5 %all-reduce.6.cloned.1.call-done = f32[64,1,2,128]{3,0,2,1:T(8,128)} async-done(((f32[64,1,2,128]{3,0,2,1:T(8,128)}), f32[64,1,2,128]{3,0,2,1:T(8,128)}) %all-reduce.6.cloned.1.call-update) | async-done | bytes 65552
  554.3 0.8 copy.577
  555.1 11.8 %all-to-all-start.1 = ((f32[2,1,2,128]{0,2,1,3:T(2,128)}), f32[2,1,2,128]{0,2,1,3:T(2,128)S(1)}, u32[]{:S(2)}, u32[]{:S(2)}) async-start(f32[2,1,2,128]{0,2,1,3:T(2,128)} %copy.577), calls=%async_computation.1 | async-start | bytes 262144 | tf_op jit(solution)/shard_map/all_to_all | solution.py:132
  567.4 8.3 %all-to-all-done.1 = f32[2,1,2,128]{0,2,1,3:T(2,128)S(1)} async-done(((f32[2,1,2,128]{0,2,1,3:T(2,128)}), f32[2,1,2,128]{0,2,1,3:T(2,128)S(1)}, u32[]{:S(2)}, u32[]{:S(2)}) %all-to-all-start.1) | async-done | bytes 2080 | tf_op jit(solution)/shard_map/all_to_all | solution.py:132
  575.9 1.0 convolution_bitcast_fusion
  (402 shorter events, 102.1 us)
Async XLA Ops:
  6.5 136.4 %copy-start = (f32[2,33,64,64]{3,2,1,0:T(8,128)S(1)}, f32[2,33,64,64]{3,2,1,0:T(8,128)}, u32[]{:S(2)}) copy-start(f32[2,33,64,64]{3,2,1,0:T(8,128)} %param.3) | copy-start | bytes 3244036
  9.3 17.6 %all-to-all-start = ((f32[2,8,2,16]{1,0,2,3:T(2,128)}), f32[2,8,2,16]{1,0,2,3:T(2,128)S(1)}, u32[]{:S(2)}, u32[]{:S(2)}) async-start(f32[2,8,2,16]{1,0,2,3:T(2,128)} %copy.367), calls=%async_computation | async-start | bytes 65536 | tf_op jit(solution)/shard_map/all_to_all | solution.py:45
  19.4 280.5 %all-reduce.4.cloned.1.call-start = ((), (), s32[]{:S(2)}) async-start(), calls=%async_computation.3 | async-start | bytes 131072 | tf_op jit(solution)/shard_map/psum | solution.py:60
  113.8 14.5 %copy-start.10 = (f32[1,1,2,33,64]{4,2,3,1,0:T(2,128)S(1)}, f32[1,1,2,33,64]{4,2,3,1,0:T(2,128)}, u32[]{:S(2)}) copy-start(f32[1,1,2,33,64]{4,2,3,1,0:T(2,128)} %get-tuple-element.145) | copy-start | bytes 50692
  114.5 14.5 %copy-start.9 = (f32[1,1,2,33,64]{4,2,3,1,0:T(2,128)S(1)}, f32[1,1,2,33,64]{4,2,3,1,0:T(2,128)}, u32[]{:S(2)}) copy-start(f32[1,1,2,33,64]{4,2,3,1,0:T(2,128)} %get-tuple-element.144) | copy-start | bytes 50692
  115.2 14.6 %copy-start.8 = (f32[1,1,2,33,64]{4,2,3,1,0:T(2,128)S(1)}, f32[1,1,2,33,64]{4,2,3,1,0:T(2,128)}, u32[]{:S(2)}) copy-start(f32[1,1,2,33,64]{4,2,3,1,0:T(2,128)} %get-tuple-element.143) | copy-start | bytes 50692
  115.9 14.5 %copy-start.7 = (f32[1,1,2,33,64]{4,2,3,1,0:T(2,128)S(1)}, f32[1,1,2,33,64]{4,2,3,1,0:T(2,128)}, u32[]{:S(2)}) copy-start(f32[1,1,2,33,64]{4,2,3,1,0:T(2,128)} %get-tuple-element.142) | copy-start | bytes 50692
  116.6 14.5 %copy-start.6 = (f32[1,1,2,33,64]{4,2,3,1,0:T(2,128)S(1)}, f32[1,1,2,33,64]{4,2,3,1,0:T(2,128)}, u32[]{:S(2)}) copy-start(f32[1,1,2,33,64]{4,2,3,1,0:T(2,128)} %get-tuple-element.141) | copy-start | bytes 50692
  117.3 14.5 %copy-start.5 = (f32[1,1,2,33,64]{4,2,3,1,0:T(2,128)S(1)}, f32[1,1,2,33,64]{4,2,3,1,0:T(2,128)}, u32[]{:S(2)}) copy-start(f32[1,1,2,33,64]{4,2,3,1,0:T(2,128)} %get-tuple-element.140) | copy-start | bytes 50692
  118.0 14.6 %copy-start.4 = (f32[1,1,2,33,64]{4,2,3,1,0:T(2,128)S(1)}, f32[1,1,2,33,64]{4,2,3,1,0:T(2,128)}, u32[]{:S(2)}) copy-start(f32[1,1,2,33,64]{4,2,3,1,0:T(2,128)} %get-tuple-element.139) | copy-start | bytes 50692
  118.7 14.5 %copy-start.3 = (f32[1,1,2,33,64]{4,2,3,1,0:T(2,128)S(1)}, f32[1,1,2,33,64]{4,2,3,1,0:T(2,128)}, u32[]{:S(2)}) copy-start(f32[1,1,2,33,64]{4,2,3,1,0:T(2,128)} %get-tuple-element.138) | copy-start | bytes 50692
  119.4 14.6 %copy-start.51 = (f32[2,1,2112]{2,1,0:T(1,128)S(1)}, f32[2,1,2112]{2,1,0:T(1,128)}, u32[]{:S(2)}) copy-start(f32[2,1,2112]{2,1,0:T(1,128)} %stack.571) | copy-start | bytes 50692
  119.4 14.6 %copy-start.52 = (f32[2,1,2112]{2,1,0:T(1,128)S(1)}, f32[2,1,2112]{2,1,0:T(1,128)}, u32[]{:S(2)}) copy-start(f32[2,1,2112]{2,1,0:T(1,128)} %stack.572) | copy-start | bytes 50692
  147.5 235.1 %all-gather.2.cloned.1.call-start = ((), (), s32[]{:S(2)}) async-start(), calls=%async_computation.2 | async-start | bytes 1098240 | tf_op jit(solution)/shard_map/all_gather | solution.py:59
  148.3 405.3 %all-reduce.6.cloned.1.call-start = ((), (), s32[]{:S(2)}) async-start(), calls=%async_computation.4 | async-start | bytes 131072
  188.1 10.6 %copy-start.11 = (f32[1,2,1,2080]{3,2,1,0:T(1,128)S(1)}, f32[1,2,1,2080]{3,2,1,0:T(1,128)}, u32[]{:S(2)}) copy-start(f32[1,2,1,2080]{3,2,1,0:T(1,128)} %stack.491) | copy-start | bytes 49924
  188.1 10.6 %copy-start.12 = (f32[1,2,1,2080]{3,2,1,0:T(1,128)S(1)}, f32[1,2,1,2080]{3,2,1,0:T(1,128)}, u32[]{:S(2)}) copy-start(f32[1,2,1,2080]{3,2,1,0:T(1,128)} %stack.508) | copy-start | bytes 49924
  188.1 10.6 %copy-start.13 = (f32[1,2,1,2080]{3,2,1,0:T(1,128)S(1)}, f32[1,2,1,2080]{3,2,1,0:T(1,128)}, u32[]{:S(2)}) copy-start(f32[1,2,1,2080]{3,2,1,0:T(1,128)} %stack.509) | copy-start | bytes 49924
  188.1 10.6 %copy-start.14 = (f32[1,2,1,2080]{3,2,1,0:T(1,128)S(1)}, f32[1,2,1,2080]{3,2,1,0:T(1,128)}, u32[]{:S(2)}) copy-start(f32[1,2,1,2080]{3,2,1,0:T(1,128)} %stack.510) | copy-start | bytes 49924
  188.2 10.6 %copy-start.15 = (f32[1,2,1,2080]{3,2,1,0:T(1,128)S(1)}, f32[1,2,1,2080]{3,2,1,0:T(1,128)}, u32[]{:S(2)}) copy-start(f32[1,2,1,2080]{3,2,1,0:T(1,128)} %stack.511) | copy-start | bytes 49924
  188.2 10.6 %copy-start.16 = (f32[1,2,1,2080]{3,2,1,0:T(1,128)S(1)}, f32[1,2,1,2080]{3,2,1,0:T(1,128)}, u32[]{:S(2)}) copy-start(f32[1,2,1,2080]{3,2,1,0:T(1,128)} %stack.512) | copy-start | bytes 49924
  188.2 10.6 %copy-start.17 = (f32[1,2,1,2080]{3,2,1,0:T(1,128)S(1)}, f32[1,2,1,2080]{3,2,1,0:T(1,128)}, u32[]{:S(2)}) copy-start(f32[1,2,1,2080]{3,2,1,0:T(1,128)} %stack.513) | copy-start | bytes 49924
  188.2 10.6 %copy-start.18 = (f32[1,2,1,2080]{3,2,1,0:T(1,128)S(1)}, f32[1,2,1,2080]{3,2,1,0:T(1,128)}, u32[]{:S(2)}) copy-start(f32[1,2,1,2080]{3,2,1,0:T(1,128)} %stack.514) | copy-start | bytes 49924
  188.2 10.6 %copy-start.19 = (f32[1,2,1,2080]{3,2,1,0:T(1,128)S(1)}, f32[1,2,1,2080]{3,2,1,0:T(1,128)}, u32[]{:S(2)}) copy-start(f32[1,2,1,2080]{3,2,1,0:T(1,128)} %stack.515) | copy-start | bytes 49924
  188.2 10.6 %copy-start.20 = (f32[1,2,1,2080]{3,2,1,0:T(1,128)S(1)}, f32[1,2,1,2080]{3,2,1,0:T(1,128)}, u32[]{:S(2)}) copy-start(f32[1,2,1,2080]{3,2,1,0:T(1,128)} %stack.516) | copy-start | bytes 49924
  188.2 10.6 %copy-start.21 = (f32[1,2,1,2080]{3,2,1,0:T(1,128)S(1)}, f32[1,2,1,2080]{3,2,1,0:T(1,128)}, u32[]{:S(2)}) copy-start(f32[1,2,1,2080]{3,2,1,0:T(1,128)} %stack.517) | copy-start | bytes 49924
  188.2 10.6 %copy-start.22 = (f32[1,2,1,2080]{3,2,1,0:T(1,128)S(1)}, f32[1,2,1,2080]{3,2,1,0:T(1,128)}, u32[]{:S(2)}) copy-start(f32[1,2,1,2080]{3,2,1,0:T(1,128)} %stack.518) | copy-start | bytes 49924
  188.2 10.6 %copy-start.23 = (f32[1,2,1,2080]{3,2,1,0:T(1,128)S(1)}, f32[1,2,1,2080]{3,2,1,0:T(1,128)}, u32[]{:S(2)}) copy-start(f32[1,2,1,2080]{3,2,1,0:T(1,128)} %stack.519) | copy-start | bytes 49924
  188.2 10.6 %copy-start.24 = (f32[1,2,1,2080]{3,2,1,0:T(1,128)S(1)}, f32[1,2,1,2080]{3,2,1,0:T(1,128)}, u32[]{:S(2)}) copy-start(f32[1,2,1,2080]{3,2,1,0:T(1,128)} %stack.520) | copy-start | bytes 49924
  188.3 10.6 %copy-start.25 = (f32[1,2,1,2080]{3,2,1,0:T(1,128)S(1)}, f32[1,2,1,2080]{3,2,1,0:T(1,128)}, u32[]{:S(2)}) copy-start(f32[1,2,1,2080]{3,2,1,0:T(1,128)} %stack.521) | copy-start | bytes 49924
  188.3 10.6 %copy-start.26 = (f32[1,2,1,2080]{3,2,1,0:T(1,128)S(1)}, f32[1,2,1,2080]{3,2,1,0:T(1,128)}, u32[]{:S(2)}) copy-start(f32[1,2,1,2080]{3,2,1,0:T(1,128)} %stack.522) | copy-start | bytes 49924
  188.3 10.6 %copy-start.27 = (f32[1,2,1,2080]{3,2,1,0:T(1,128)S(1)}, f32[1,2,1,2080]{3,2,1,0:T(1,128)}, u32[]{:S(2)}) copy-start(f32[1,2,1,2080]{3,2,1,0:T(1,128)} %stack.523) | copy-start | bytes 49924
  188.3 10.6 %copy-start.28 = (f32[1,2,1,2080]{3,2,1,0:T(1,128)S(1)}, f32[1,2,1,2080]{3,2,1,0:T(1,128)}, u32[]{:S(2)}) copy-start(f32[1,2,1,2080]{3,2,1,0:T(1,128)} %stack.492) | copy-start | bytes 49924
  188.3 10.6 %copy-start.29 = (f32[1,2,1,2080]{3,2,1,0:T(1,128)S(1)}, f32[1,2,1,2080]{3,2,1,0:T(1,128)}, u32[]{:S(2)}) copy-start(f32[1,2,1,2080]{3,2,1,0:T(1,128)} %stack.493) | copy-start | bytes 49924
  188.3 10.6 %copy-start.30 = (f32[1,2,1,2080]{3,2,1,0:T(1,128)S(1)}, f32[1,2,1,2080]{3,2,1,0:T(1,128)}, u32[]{:S(2)}) copy-start(f32[1,2,1,2080]{3,2,1,0:T(1,128)} %stack.494) | copy-start | bytes 49924
  188.3 10.6 %copy-start.31 = (f32[1,2,1,2080]{3,2,1,0:T(1,128)S(1)}, f32[1,2,1,2080]{3,2,1,0:T(1,128)}, u32[]{:S(2)}) copy-start(f32[1,2,1,2080]{3,2,1,0:T(1,128)} %stack.495) | copy-start | bytes 49924
  188.3 10.6 %copy-start.32 = (f32[1,2,1,2080]{3,2,1,0:T(1,128)S(1)}, f32[1,2,1,2080]{3,2,1,0:T(1,128)}, u32[]{:S(2)}) copy-start(f32[1,2,1,2080]{3,2,1,0:T(1,128)} %stack.496) | copy-start | bytes 49924
  188.3 10.6 %copy-start.33 = (f32[1,2,1,2080]{3,2,1,0:T(1,128)S(1)}, f32[1,2,1,2080]{3,2,1,0:T(1,128)}, u32[]{:S(2)}) copy-start(f32[1,2,1,2080]{3,2,1,0:T(1,128)} %stack.497) | copy-start | bytes 49924
  188.3 10.6 %copy-start.34 = (f32[1,2,1,2080]{3,2,1,0:T(1,128)S(1)}, f32[1,2,1,2080]{3,2,1,0:T(1,128)}, u32[]{:S(2)}) copy-start(f32[1,2,1,2080]{3,2,1,0:T(1,128)} %stack.498) | copy-start | bytes 49924
  188.4 10.6 %copy-start.35 = (f32[1,2,1,2080]{3,2,1,0:T(1,128)S(1)}, f32[1,2,1,2080]{3,2,1,0:T(1,128)}, u32[]{:S(2)}) copy-start(f32[1,2,1,2080]{3,2,1,0:T(1,128)} %stack.499) | copy-start | bytes 49924
  188.4 10.6 %copy-start.36 = (f32[1,2,1,2080]{3,2,1,0:T(1,128)S(1)}, f32[1,2,1,2080]{3,2,1,0:T(1,128)}, u32[]{:S(2)}) copy-start(f32[1,2,1,2080]{3,2,1,0:T(1,128)} %stack.500) | copy-start | bytes 49924
  194.6 10.0 %copy-start.41 = (f32[1,2,1,2080]{3,2,1,0:T(1,128)S(1)}, f32[1,2,1,2080]{3,2,1,0:T(1,128)}, u32[]{:S(2)}) copy-start(f32[1,2,1,2080]{3,2,1,0:T(1,128)} %stack.545) | copy-start | bytes 49924
  194.6 10.0 %copy-start.42 = (f32[1,2,1,2080]{3,2,1,0:T(1,128)S(1)}, f32[1,2,1,2080]{3,2,1,0:T(1,128)}, u32[]{:S(2)}) copy-start(f32[1,2,1,2080]{3,2,1,0:T(1,128)} %stack.546) | copy-start | bytes 49924
  194.6 10.0 %copy-start.43 = (f32[1,2,1,2080]{3,2,1,0:T(1,128)S(1)}, f32[1,2,1,2080]{3,2,1,0:T(1,128)}, u32[]{:S(2)}) copy-start(f32[1,2,1,2080]{3,2,1,0:T(1,128)} %stack.547) | copy-start | bytes 49924
  194.6 10.0 %copy-start.44 = (f32[1,2,1,2080]{3,2,1,0:T(1,128)S(1)}, f32[1,2,1,2080]{3,2,1,0:T(1,128)}, u32[]{:S(2)}) copy-start(f32[1,2,1,2080]{3,2,1,0:T(1,128)} %stack.548) | copy-start | bytes 49924
  194.6 10.0 %copy-start.45 = (f32[1,2,1,2080]{3,2,1,0:T(1,128)S(1)}, f32[1,2,1,2080]{3,2,1,0:T(1,128)}, u32[]{:S(2)}) copy-start(f32[1,2,1,2080]{3,2,1,0:T(1,128)} %stack.549) | copy-start | bytes 49924
  397.8 169.1 %copy-start.54 = (s32[16]{0:T(128)S(1)}, s32[16]{0:T(128)}, u32[]{:S(2)}) copy-start(s32[16]{0:T(128)} %copy-done.53) | copy-start | bytes 196
  555.1 20.7 %all-to-all-start.1 = ((f32[2,1,2,128]{0,2,1,3:T(2,128)}), f32[2,1,2,128]{0,2,1,3:T(2,128)S(1)}, u32[]{:S(2)}, u32[]{:S(2)}) async-start(f32[2,1,2,128]{0,2,1,3:T(2,128)} %copy.577), calls=%async_computation.1 | async-start | bytes 262144 | tf_op jit(solution)/shard_map/all_to_all | solution.py:132
  (14 other events, 99.3 us)
Sparse Core Ops, SparseCore 0:
  147.6 152.2 all-reduce.3
  303.1 79.4 all-gather.1
  402.2 151.3 all-reduce.5
where the time goes:
time: 587 us; the launch traced here: 583 us
  waiting for transfers between devices  313 us (53%)
  local copies, waits for them, and re-layouts  147 us (25%)
  blocking collectives  41.2 us (7%)
  other arithmetic  27.8 us (5%)
  starting transfers between devices  22.2 us (4%)
  matrix products  18.2 us (3%)
  between operations  14.9 us (3%)
    unnamed x4, waiting for transfers between devices  150 us
    psum x1, waiting for transfers between devices, body(): lax.psum(jnp.einsum('afbp,afbq->fpq', own_sketch, own_sketch, precision=h...  89 us
    all_gather x1, waiting for transfers between devices, body(): sketch = lax.all_gather(own_sketch, 'trace', axis=0, tiled=True)  58.3 us
    another operation x66, local copies, waits for them, and re-layouts, body(): jnp.stack([row_slabs[..., anchor:anchor + lag_y] for anchor in range(win_...  53 us
    another operation x68, local copies, waits for them, and re-layouts, body(): jnp.stack([band[:, :, anchor:anchor + win_x] for anchor in range(lag_x)],...  51 us
    all_gather x1, blocking collectives, body(): whole_slices = lax.all_gather(slices, 'trace', axis=2, tiled=True)  41.2 us
    slice x69, local copies, waits for them, and re-layouts, body(): row_slabs[..., anchor:anchor + lag_y]  21.6 us
    another operation x3, other arithmetic, body(): factor = jnp.linalg.cholesky(real_gram)  12.6 us
  transfers between devices with their start and end apart: 5, of which 5 were waited for; matrix products, arithmetic and copies ran while one was open for 15% of the time, Pallas kernels for 0%

commit v1 on v0

--- a/solution.py
+++ b/solution.py
@@ -44,7 +44,9 @@
     spectrum = jnp.einsum("xyt,tpk->xypk", traces.astype(jnp.float32), forward, precision=highest)
     spectrum = lax.all_to_all(spectrum, "freq", split_axis=3, concat_axis=1, tiled=True)
     slices = jnp.transpose(spectrum, (3, 2, 0, 1))
-    whole_slices = lax.all_gather(slices, "trace", axis=2, tiled=True)
+    whole_slices = jnp.concatenate(
+        lax.all_to_all(jnp.stack([slices] * lax.axis_size("trace")), "trace", 0, 0), axis=2
+    )
     freq_dev = whole_slices.shape[0]
     first_row = position * own_rows
     row_slabs = jnp.stack([lax.dynamic_slice_in_dim(whole_slices, first_row + 0, lag_x, 2)], axis=1)

time: 587 us -> 561 us (0.956)
  blocking collectives: 41.2 us -> 16.7 us
  waiting for transfers between devices: 313 us -> 295 us
  local copies, waits for them, and re-layouts: 147 us -> 161 us
    all_gather x1 -> x0, blocking collectives: 41.2 us -> none  [body(): whole_slices = lax.all_gather(slices, 'trace', axis=2, tiled=True)]
    another operation x66, local copies, waits for them, and re-layouts: 53 us -> 79.2 us  [body(): jnp.stack([row_slabs[..., anchor:anchor + lag_y] for anchor in range(win_...]
    psum x1, waiting for transfers between devices: 89 us -> 69.7 us  [body(): lax.psum(jnp.einsum('afbp,afbq->fpq', own_sketch, own_sketch, precision=h...]
    slice x69 -> x4, local copies, waits for them, and re-layouts: 21.6 us -> 2.58 us  [body(): row_slabs[..., anchor:anchor + lag_y]]
    all_to_all x0 -> x1, blocking collectives: none -> 16.7 us  [body(): lax.all_to_all(spectrum, 'freq', split_axis=3, concat_axis=1, tiled=True)]
    another operation x68, local copies, waits for them, and re-layouts: 51 us -> 65.9 us  [body(): jnp.stack([band[:, :, anchor:anchor + win_x] for anchor in range(lag_x)],...]
    slice x68 -> x2, local copies, waits for them, and re-layouts: 9.33 us -> 1.47 us  [body(): band[:, :, anchor:anchor + win_x]]
  transfers between devices with their start and end apart: 5 -> 5, of which waited for: 5 -> 5; matrix products, arithmetic and copies ran while one was open for 15% -> 17% of each run, Pallas kernels for 0% -> 0%
where the time goes in v1:
time: 561 us; the launch traced here: 557 us
  waiting for transfers between devices  295 us (53%)
  local copies, waits for them, and re-layouts  161 us (29%)
  other arithmetic  27.7 us (5%)
  starting transfers between devices  24 us (4%)
  matrix products  18.2 us (3%)
  blocking collectives  16.7 us (3%)
  between operations  14.5 us (3%)
    unnamed x4, waiting for transfers between devices  149 us
    another operation x66, local copies, waits for them, and re-layouts, body(): jnp.stack([row_slabs[..., anchor:anchor + lag_y] for anchor in range(win_...  79.2 us
    psum x1, waiting for transfers between devices, body(): lax.psum(jnp.einsum('afbp,afbq->fpq', own_sketch, own_sketch, precision=h...  69.7 us
    another operation x68, local copies, waits for them, and re-layouts, body(): jnp.stack([band[:, :, anchor:anchor + win_x] for anchor in range(lag_x)],...  65.9 us
    all_gather x1, waiting for transfers between devices, body(): sketch = lax.all_gather(own_sketch, 'trace', axis=0, tiled=True)  58.6 us
    all_to_all x1, blocking collectives, body(): lax.all_to_all(spectrum, 'freq', split_axis=3, concat_axis=1, tiled=True)  16.7 us
    another operation x3, other arithmetic, body(): factor = jnp.linalg.cholesky(real_gram)  12.5 us
    all_to_all x1, starting transfers between devices, body(): lax.all_to_all(jnp.stack([slices] * lax.axis_size('trace')), 'trace', 0, 0)  12 us
  transfers between devices with their start and end apart: 5, of which 5 were waited for; matrix products, arithmetic and copies ran while one was open for 17% of the time, Pallas kernels for 0%

profile of v1, /device:TPU:1, one launch (start us, length us, event | category | flops | bytes accessed | tf_op | source)
XLA Modules:
  0.0 556.7 jit_solution(11808364178098569090)
XLA Ops:
  8.7 16.7 %all_to_all.41 = f32[2,8,2,16]{1,0,2,3:T(2,128)S(1)} all-to-all(f32[2,8,2,16]{1,0,2,3:T(2,128)S(1)} %copy.174), channel_id=1, replica_groups=mesh['freq'=16,'trace'=32] {'freq'}, dimensions={3} | all-to-all | bytes 4096 | tf_op jit(solution)/shard_map/all_to_all | solution.py:45
  26.2 12.0 %all-to-all-start.1 = ((f32[32,1,2,2,128]{4,3,2,1,0:T(2,128)}), f32[32,1,2,2,128]{4,3,2,1,0:T(2,128)S(1)}, u32[]{:S(2)}, u32[]{:S(2)}) async-start(f32[32,1,2,2,128]{4,3,2,1,0:T(2,128)} %stack.459), calls=%async_computation.1 | async-start | bytes 131072 | tf_op jit(solution)/shard_map/all_to_all | solution.py:48
  38.2 8.8 %all-to-all-done.1 = f32[32,1,2,2,128]{4,3,2,1,0:T(2,128)S(1)} async-done(((f32[32,1,2,2,128]{4,3,2,1,0:T(2,128)}), f32[32,1,2,2,128]{4,3,2,1,0:T(2,128)S(1)}, u32[]{:S(2)}, u32[]{:S(2)}) %all-to-all-start.1) | async-done | bytes 65568 | tf_op jit(solution)/shard_map/all_to_all | solution.py:48
  49.6 1.5 stack.606
  51.1 1.5 stack.607
  54.0 1.5 stack.609
  55.5 1.5 stack.610
  59.8 1.5 stack.613
  64.2 1.5 stack.616
  65.7 1.5 stack.617
  67.2 1.5 stack.618
  70.1 1.5 stack.620
  71.5 1.5 stack.621
  73.0 1.5 stack.622
  75.9 1.5 stack.624
  78.9 1.5 stack.626
  81.8 1.5 stack.628
  83.2 1.5 stack.629
  86.2 1.5 stack.631
  87.6 1.5 stack.632
  90.6 1.5 stack.634
  92.0 1.5 stack.635
  93.5 1.5 stack.636
  96.4 1.5 stack.638
  119.8 9.0 %stack.526 = f32[2,65,2112]{2,1,0:T(8,128)S(1)} concatenate(f32[2,1,2112]{2,1,0:T(1,128)} %stack.598, f32[2,1,2112]{2,1,0:T(1,128)} %stack.599, f32[2,1,2112]{2,1,0:T(1,128)} %stack.600, f32[2,1,2112]{2,1,0:T(1,128)} %stack.601, f32[2,1,2112]{2,1,0:T(1,128)} %stack.602, f32[2,1,2112]{2,1,0:T(1,128)} %stack.603, f32[2,1,2112]{2,1,0:T(1,128)} %stack.604, f32[2,1,2112]{2,1,0:T(1,128)} %stack.605, ...), dimensions={1} | concatenate | bytes 2196480 | tf_op jit(solution)/shard_map/stack | solution.py:53
  128.8 3.6 fusion.6
  149.3 1.5 stack.528
  150.8 1.5 stack.529
  152.3 1.5 stack.530
  153.8 1.5 stack.531
  155.2 1.5 stack.532
  156.7 1.5 stack.533
  158.2 1.5 stack.534
  159.6 1.5 stack.535
  161.1 1.5 stack.536
  189.8 7.1 %stack.560 = f32[1,2,33,2080]{3,2,1,0:T(8,128)} concatenate(f32[1,2,1,2080]{3,2,1,0:T(1,128)S(1)} %copy-done.3, f32[1,2,1,2080]{3,2,1,0:T(1,128)S(1)} %copy-done.6, f32[1,2,1,2080]{3,2,1,0:T(1,128)S(1)} %copy-done.7, f32[1,2,1,2080]{3,2,1,0:T(1,128)S(1)} %copy-done.8, f32[1,2,1,2080]{3,2,1,0:T(1,128)S(1)} %copy-done.9, f32[1,2,1,2080]{3,2,1,0:T(1,128)S(1)} %copy-done.10, ...), dimensions={2} | concatenate | bytes 1098240 | tf_op jit(solution)/shard_map/stack | solution.py:70
  197.1 6.3 %stack.594 = f32[1,2,33,2080]{3,2,1,0:T(8,128)} concatenate(f32[1,2,1,2080]{3,2,1,0:T(1,128)} %stack.561, f32[1,2,1,2080]{3,2,1,0:T(1,128)S(1)} %copy-done.34, f32[1,2,1,2080]{3,2,1,0:T(1,128)S(1)} %copy-done.35, f32[1,2,1,2080]{3,2,1,0:T(1,128)S(1)} %copy-done.36, f32[1,2,1,2080]{3,2,1,0:T(1,128)S(1)} %copy-done.37, f32[1,2,1,2080]{3,2,1,0:T(1,128)S(1)} %copy-done.38, ...), dimensions={2} | concatenate | bytes 1098240 | tf_op jit(solution)/shard_map/stack | solution.py:70
  203.5 69.7 %all-reduce.4.cloned.1.call-done = f32[1,128,128]{1,2,0:T(8,128)} async-done(((f32[1,128,128]{1,2,0:T(8,128)}), f32[1,128,128]{1,2,0:T(8,128)}) %all-reduce.4.cloned.1.call-update) | async-done | bytes 65552 | tf_op jit(solution)/shard_map/psum | solution.py:62
  274.3 11.9 %custom-call.11 = f32[1,128,128]{2,1,0:T(8,128)S(1)} custom-call(f32[1,128,128]{2,1,0:T(8,128)S(1)} %fusion.46), custom_call_target="Cholesky" | custom-call | tf_op jit(solution)/shard_map/jit(cholesky)/cholesky | solution.py:95
  287.5 9.8 %custom-call.12 = f32[1,1,128,128]{2,3,1,0:T(8,128)S(1)} custom-call(f32[1,1,128,128]{3,2,1,0:T(8,128)S(1)} %fusion.41), custom_call_target="InvertDiagBlocksLowerTriangular" | custom-call | tf_op jit(solution)/shard_map/vmap(jit(_cho_solve))/triangular_solve | solution.py:25
  297.3 58.6 %all-gather.2.cloned.1.call-done = f32[32,1,65,128]{3,1,2,0:T(1,128)} async-done(((f32[1,1,65,128]{3,1,2,0:T(1,128)}), f32[32,1,65,128]{3,1,2,0:T(1,128)}) %all-gather.2.cloned.1.call-update) | async-done | bytes 1064976 | tf_op jit(solution)/shard_map/all_gather | solution.py:61
  355.9 3.1 fusion.9
  360.0 5.1 convolution_bitcast_fusion.1
  365.1 6.0 %copy.252 = f32[1,65,2,2,33,32]{1,5,4,3,2,0:T(8,128)} copy(f32[1,65,2,2,33,32]{4,5,3,2,1,0:T(8,128)} %convolution_bitcast_fusion.1) | data formatting | bytes 2196480 | tf_op jit(solution)/shard_map/fqezc,fbqa->fbezca/transpose | solution.py:107
  371.1 2.6 convolution_bitcast_fusion.2
  377.4 149.4 %all-reduce.6.cloned.1.call-done = f32[64,1,2,128]{3,0,2,1:T(8,128)} async-done(((f32[64,1,2,128]{3,0,2,1:T(8,128)}), f32[64,1,2,128]{3,0,2,1:T(8,128)}) %all-reduce.6.cloned.1.call-update) | async-done | bytes 65552
  528.4 11.8 %all-to-all-start.2 = ((f32[2,1,2,128]{0,2,1,3:T(2,128)}), f32[2,1,2,128]{0,2,1,3:T(2,128)S(1)}, u32[]{:S(2)}, u32[]{:S(2)}) async-start(f32[2,1,2,128]{0,2,1,3:T(2,128)} %copy.254), calls=%async_computation.2 | async-start | bytes 262144 | tf_op jit(solution)/shard_map/all_to_all | solution.py:134
  540.8 8.3 %all-to-all-done.2 = f32[2,1,2,128]{0,2,1,3:T(2,128)S(1)} async-done(((f32[2,1,2,128]{0,2,1,3:T(2,128)}), f32[2,1,2,128]{0,2,1,3:T(2,128)S(1)}, u32[]{:S(2)}, u32[]{:S(2)}) %all-to-all-start.2) | async-done | bytes 2080 | tf_op jit(solution)/shard_map/all_to_all | solution.py:134
  (258 shorter events, 98.6 us)
Async XLA Ops:
  6.5 122.3 %copy-start = (f32[2,33,64,64]{3,2,1,0:T(8,128)S(1)}, f32[2,33,64,64]{3,2,1,0:T(8,128)}, u32[]{:S(2)}) copy-start(f32[2,33,64,64]{3,2,1,0:T(8,128)} %param.3) | copy-start | bytes 3244036
  26.2 20.8 %all-to-all-start.1 = ((f32[32,1,2,2,128]{4,3,2,1,0:T(2,128)}), f32[32,1,2,2,128]{4,3,2,1,0:T(2,128)S(1)}, u32[]{:S(2)}, u32[]{:S(2)}) async-start(f32[32,1,2,2,128]{4,3,2,1,0:T(2,128)} %stack.459), calls=%async_computation.1 | async-start | bytes 131072 | tf_op jit(solution)/shard_map/all_to_all | solution.py:48
  38.1 235.0 %all-reduce.4.cloned.1.call-start = ((), (), s32[]{:S(2)}) async-start(), calls=%async_computation.4 | async-start | bytes 131072 | tf_op jit(solution)/shard_map/psum | solution.py:62
  98.6 21.3 %copy-start.43 = (f32[2,1,2112]{2,1,0:T(1,128)S(1)}, f32[2,1,2112]{2,1,0:T(1,128)}, u32[]{:S(2)}) copy-start(f32[2,1,2112]{2,1,0:T(1,128)} %stack.606) | copy-start | bytes 50692
  98.6 21.3 %copy-start.44 = (f32[2,1,2112]{2,1,0:T(1,128)S(1)}, f32[2,1,2112]{2,1,0:T(1,128)}, u32[]{:S(2)}) copy-start(f32[2,1,2112]{2,1,0:T(1,128)} %stack.607) | copy-start | bytes 50692
  133.4 222.5 %all-gather.2.cloned.1.call-start = ((), (), s32[]{:S(2)}) async-start(), calls=%async_computation.3 | async-start | bytes 1098240 | tf_op jit(solution)/shard_map/all_gather | solution.py:61
  134.2 392.7 %all-reduce.6.cloned.1.call-start = ((), (), s32[]{:S(2)}) async-start(), calls=%async_computation.5 | async-start | bytes 131072
  149.3 40.3 %copy-start.3 = (f32[1,2,1,2080]{3,2,1,0:T(1,128)S(1)}, f32[1,2,1,2080]{3,2,1,0:T(1,128)}, u32[]{:S(2)}) copy-start(f32[1,2,1,2080]{3,2,1,0:T(1,128)} %stack.527) | copy-start | bytes 49924
  149.3 40.3 %copy-start.4 = (f32[1,2,1,2080]{3,2,1,0:T(1,128)S(1)}, f32[1,2,1,2080]{3,2,1,0:T(1,128)}, u32[]{:S(2)}) copy-start(f32[1,2,1,2080]{3,2,1,0:T(1,128)} %stack.544) | copy-start | bytes 49924
  149.3 40.3 %copy-start.5 = (f32[1,2,1,2080]{3,2,1,0:T(1,128)S(1)}, f32[1,2,1,2080]{3,2,1,0:T(1,128)}, u32[]{:S(2)}) copy-start(f32[1,2,1,2080]{3,2,1,0:T(1,128)} %stack.545) | copy-start | bytes 49924
  163.3 26.3 %copy-start.6 = (f32[1,2,1,2080]{3,2,1,0:T(1,128)S(1)}, f32[1,2,1,2080]{3,2,1,0:T(1,128)}, u32[]{:S(2)}) copy-start(f32[1,2,1,2080]{3,2,1,0:T(1,128)} %stack.528) | copy-start | bytes 49924
  163.3 26.3 %copy-start.7 = (f32[1,2,1,2080]{3,2,1,0:T(1,128)S(1)}, f32[1,2,1,2080]{3,2,1,0:T(1,128)}, u32[]{:S(2)}) copy-start(f32[1,2,1,2080]{3,2,1,0:T(1,128)} %stack.529) | copy-start | bytes 49924
  164.0 25.6 %copy-start.8 = (f32[1,2,1,2080]{3,2,1,0:T(1,128)S(1)}, f32[1,2,1,2080]{3,2,1,0:T(1,128)}, u32[]{:S(2)}) copy-start(f32[1,2,1,2080]{3,2,1,0:T(1,128)} %stack.530) | copy-start | bytes 49924
  164.7 24.9 %copy-start.9 = (f32[1,2,1,2080]{3,2,1,0:T(1,128)S(1)}, f32[1,2,1,2080]{3,2,1,0:T(1,128)}, u32[]{:S(2)}) copy-start(f32[1,2,1,2080]{3,2,1,0:T(1,128)} %stack.531) | copy-start | bytes 49924
  165.5 24.2 %copy-start.10 = (f32[1,2,1,2080]{3,2,1,0:T(1,128)S(1)}, f32[1,2,1,2080]{3,2,1,0:T(1,128)}, u32[]{:S(2)}) copy-start(f32[1,2,1,2080]{3,2,1,0:T(1,128)} %stack.532) | copy-start | bytes 49924
  166.2 23.5 %copy-start.11 = (f32[1,2,1,2080]{3,2,1,0:T(1,128)S(1)}, f32[1,2,1,2080]{3,2,1,0:T(1,128)}, u32[]{:S(2)}) copy-start(f32[1,2,1,2080]{3,2,1,0:T(1,128)} %stack.533) | copy-start | bytes 49924
  166.9 22.8 %copy-start.12 = (f32[1,2,1,2080]{3,2,1,0:T(1,128)S(1)}, f32[1,2,1,2080]{3,2,1,0:T(1,128)}, u32[]{:S(2)}) copy-start(f32[1,2,1,2080]{3,2,1,0:T(1,128)} %stack.534) | copy-start | bytes 49924
  167.6 22.1 %copy-start.13 = (f32[1,2,1,2080]{3,2,1,0:T(1,128)S(1)}, f32[1,2,1,2080]{3,2,1,0:T(1,128)}, u32[]{:S(2)}) copy-start(f32[1,2,1,2080]{3,2,1,0:T(1,128)} %stack.535) | copy-start | bytes 49924
  168.3 21.4 %copy-start.14 = (f32[1,2,1,2080]{3,2,1,0:T(1,128)S(1)}, f32[1,2,1,2080]{3,2,1,0:T(1,128)}, u32[]{:S(2)}) copy-start(f32[1,2,1,2080]{3,2,1,0:T(1,128)} %stack.536) | copy-start | bytes 49924
  169.1 20.6 %copy-start.15 = (f32[1,2,1,2080]{3,2,1,0:T(1,128)S(1)}, f32[1,2,1,2080]{3,2,1,0:T(1,128)}, u32[]{:S(2)}) copy-start(f32[1,2,1,2080]{3,2,1,0:T(1,128)} %stack.537) | copy-start | bytes 49924
  169.8 19.9 %copy-start.16 = (f32[1,2,1,2080]{3,2,1,0:T(1,128)S(1)}, f32[1,2,1,2080]{3,2,1,0:T(1,128)}, u32[]{:S(2)}) copy-start(f32[1,2,1,2080]{3,2,1,0:T(1,128)} %stack.538) | copy-start | bytes 49924
  170.5 19.2 %copy-start.17 = (f32[1,2,1,2080]{3,2,1,0:T(1,128)S(1)}, f32[1,2,1,2080]{3,2,1,0:T(1,128)}, u32[]{:S(2)}) copy-start(f32[1,2,1,2080]{3,2,1,0:T(1,128)} %stack.539) | copy-start | bytes 49924
  171.2 18.5 %copy-start.18 = (f32[1,2,1,2080]{3,2,1,0:T(1,128)S(1)}, f32[1,2,1,2080]{3,2,1,0:T(1,128)}, u32[]{:S(2)}) copy-start(f32[1,2,1,2080]{3,2,1,0:T(1,128)} %stack.540) | copy-start | bytes 49924
  172.0 17.8 %copy-start.19 = (f32[1,2,1,2080]{3,2,1,0:T(1,128)S(1)}, f32[1,2,1,2080]{3,2,1,0:T(1,128)}, u32[]{:S(2)}) copy-start(f32[1,2,1,2080]{3,2,1,0:T(1,128)} %stack.541) | copy-start | bytes 49924
  172.7 24.2 %copy-start.20 = (f32[1,2,1,2080]{3,2,1,0:T(1,128)S(1)}, f32[1,2,1,2080]{3,2,1,0:T(1,128)}, u32[]{:S(2)}) copy-start(f32[1,2,1,2080]{3,2,1,0:T(1,128)} %stack.580) | copy-start | bytes 49924
  173.4 23.5 %copy-start.21 = (f32[1,2,1,2080]{3,2,1,0:T(1,128)S(1)}, f32[1,2,1,2080]{3,2,1,0:T(1,128)}, u32[]{:S(2)}) copy-start(f32[1,2,1,2080]{3,2,1,0:T(1,128)} %stack.581) | copy-start | bytes 49924
  174.1 22.8 %copy-start.22 = (f32[1,2,1,2080]{3,2,1,0:T(1,128)S(1)}, f32[1,2,1,2080]{3,2,1,0:T(1,128)}, u32[]{:S(2)}) copy-start(f32[1,2,1,2080]{3,2,1,0:T(1,128)} %stack.582) | copy-start | bytes 49924
  174.8 22.1 %copy-start.23 = (f32[1,2,1,2080]{3,2,1,0:T(1,128)S(1)}, f32[1,2,1,2080]{3,2,1,0:T(1,128)}, u32[]{:S(2)}) copy-start(f32[1,2,1,2080]{3,2,1,0:T(1,128)} %stack.583) | copy-start | bytes 49924
  175.6 21.4 %copy-start.24 = (f32[1,2,1,2080]{3,2,1,0:T(1,128)S(1)}, f32[1,2,1,2080]{3,2,1,0:T(1,128)}, u32[]{:S(2)}) copy-start(f32[1,2,1,2080]{3,2,1,0:T(1,128)} %stack.584) | copy-start | bytes 49924
  176.3 20.7 %copy-start.25 = (f32[1,2,1,2080]{3,2,1,0:T(1,128)S(1)}, f32[1,2,1,2080]{3,2,1,0:T(1,128)}, u32[]{:S(2)}) copy-start(f32[1,2,1,2080]{3,2,1,0:T(1,128)} %stack.585) | copy-start | bytes 49924
  177.0 20.0 %copy-start.26 = (f32[1,2,1,2080]{3,2,1,0:T(1,128)S(1)}, f32[1,2,1,2080]{3,2,1,0:T(1,128)}, u32[]{:S(2)}) copy-start(f32[1,2,1,2080]{3,2,1,0:T(1,128)} %stack.586) | copy-start | bytes 49924
  177.7 19.3 %copy-start.27 = (f32[1,2,1,2080]{3,2,1,0:T(1,128)S(1)}, f32[1,2,1,2080]{3,2,1,0:T(1,128)}, u32[]{:S(2)}) copy-start(f32[1,2,1,2080]{3,2,1,0:T(1,128)} %stack.587) | copy-start | bytes 49924
  178.4 18.5 %copy-start.28 = (f32[1,2,1,2080]{3,2,1,0:T(1,128)S(1)}, f32[1,2,1,2080]{3,2,1,0:T(1,128)}, u32[]{:S(2)}) copy-start(f32[1,2,1,2080]{3,2,1,0:T(1,128)} %stack.588) | copy-start | bytes 49924
  179.1 17.8 %copy-start.29 = (f32[1,2,1,2080]{3,2,1,0:T(1,128)S(1)}, f32[1,2,1,2080]{3,2,1,0:T(1,128)}, u32[]{:S(2)}) copy-start(f32[1,2,1,2080]{3,2,1,0:T(1,128)} %stack.589) | copy-start | bytes 49924
  179.9 17.1 %copy-start.30 = (f32[1,2,1,2080]{3,2,1,0:T(1,128)S(1)}, f32[1,2,1,2080]{3,2,1,0:T(1,128)}, u32[]{:S(2)}) copy-start(f32[1,2,1,2080]{3,2,1,0:T(1,128)} %stack.590) | copy-start | bytes 49924
  180.6 16.4 %copy-start.31 = (f32[1,2,1,2080]{3,2,1,0:T(1,128)S(1)}, f32[1,2,1,2080]{3,2,1,0:T(1,128)}, u32[]{:S(2)}) copy-start(f32[1,2,1,2080]{3,2,1,0:T(1,128)} %stack.591) | copy-start | bytes 49924
  181.3 15.7 %copy-start.32 = (f32[1,2,1,2080]{3,2,1,0:T(1,128)S(1)}, f32[1,2,1,2080]{3,2,1,0:T(1,128)}, u32[]{:S(2)}) copy-start(f32[1,2,1,2080]{3,2,1,0:T(1,128)} %stack.592) | copy-start | bytes 49924
  182.0 15.0 %copy-start.33 = (f32[1,2,1,2080]{3,2,1,0:T(1,128)S(1)}, f32[1,2,1,2080]{3,2,1,0:T(1,128)}, u32[]{:S(2)}) copy-start(f32[1,2,1,2080]{3,2,1,0:T(1,128)} %stack.593) | copy-start | bytes 49924
  182.8 14.3 %copy-start.34 = (f32[1,2,1,2080]{3,2,1,0:T(1,128)S(1)}, f32[1,2,1,2080]{3,2,1,0:T(1,128)}, u32[]{:S(2)}) copy-start(f32[1,2,1,2080]{3,2,1,0:T(1,128)} %stack.562) | copy-start | bytes 49924
  183.5 13.6 %copy-start.35 = (f32[1,2,1,2080]{3,2,1,0:T(1,128)S(1)}, f32[1,2,1,2080]{3,2,1,0:T(1,128)}, u32[]{:S(2)}) copy-start(f32[1,2,1,2080]{3,2,1,0:T(1,128)} %stack.563) | copy-start | bytes 49924
  184.2 12.8 %copy-start.36 = (f32[1,2,1,2080]{3,2,1,0:T(1,128)S(1)}, f32[1,2,1,2080]{3,2,1,0:T(1,128)}, u32[]{:S(2)}) copy-start(f32[1,2,1,2080]{3,2,1,0:T(1,128)} %stack.564) | copy-start | bytes 49924
  184.9 12.1 %copy-start.37 = (f32[1,2,1,2080]{3,2,1,0:T(1,128)S(1)}, f32[1,2,1,2080]{3,2,1,0:T(1,128)}, u32[]{:S(2)}) copy-start(f32[1,2,1,2080]{3,2,1,0:T(1,128)} %stack.565) | copy-start | bytes 49924
  185.6 11.4 %copy-start.38 = (f32[1,2,1,2080]{3,2,1,0:T(1,128)S(1)}, f32[1,2,1,2080]{3,2,1,0:T(1,128)}, u32[]{:S(2)}) copy-start(f32[1,2,1,2080]{3,2,1,0:T(1,128)} %stack.566) | copy-start | bytes 49924
  186.4 10.7 %copy-start.39 = (f32[1,2,1,2080]{3,2,1,0:T(1,128)S(1)}, f32[1,2,1,2080]{3,2,1,0:T(1,128)}, u32[]{:S(2)}) copy-start(f32[1,2,1,2080]{3,2,1,0:T(1,128)} %stack.567) | copy-start | bytes 49924
  187.1 10.0 %copy-start.40 = (f32[1,2,1,2080]{3,2,1,0:T(1,128)S(1)}, f32[1,2,1,2080]{3,2,1,0:T(1,128)}, u32[]{:S(2)}) copy-start(f32[1,2,1,2080]{3,2,1,0:T(1,128)} %stack.568) | copy-start | bytes 49924
  187.8 9.3 %copy-start.41 = (f32[1,2,1,2080]{3,2,1,0:T(1,128)S(1)}, f32[1,2,1,2080]{3,2,1,0:T(1,128)}, u32[]{:S(2)}) copy-start(f32[1,2,1,2080]{3,2,1,0:T(1,128)} %stack.569) | copy-start | bytes 49924
  371.1 169.1 %copy-start.46 = (s32[16]{0:T(128)S(1)}, s32[16]{0:T(128)}, u32[]{:S(2)}) copy-start(s32[16]{0:T(128)} %copy-done.45) | copy-start | bytes 196
  528.4 20.7 %all-to-all-start.2 = ((f32[2,1,2,128]{0,2,1,3:T(2,128)}), f32[2,1,2,128]{0,2,1,3:T(2,128)S(1)}, u32[]{:S(2)}, u32[]{:S(2)}) async-start(f32[2,1,2,128]{0,2,1,3:T(2,128)} %copy.254), calls=%async_computation.2 | async-start | bytes 262144 | tf_op jit(solution)/shard_map/all_to_all | solution.py:134
  (6 other events, 22.5 us)
Sparse Core Ops, SparseCore 0:
  133.5 139.5 all-reduce.3
  276.3 79.5 all-gather.1
  375.5 151.3 all-reduce.5
